TPU v7x, 128 devices: a whole 4x4x4 slice. The times are simulated.
128 devices in a mesh: sect: 4 (over y), blk: 32 (over x, z, core).
Axes of the slice: x: 4, y: 4, z: 4, core: 2. Of those that a mesh axis runs over, the one named last changes fastest.
Arguments:
- theta: bfloat16 [4, 4096, 2048], P('sect', 'blk'), may hold values from -6 to 6
- left_env: bfloat16 [4, 8, 4096, 4096], P('sect', None, 'blk'), may hold values from -0.125 to 0.125
- sector_ids: int32 [4, 4096], P('sect'), may hold values from 0 to 15, never falling along the last dimension, each value on 1 to 2560 neighbouring positions
- local_ops: float32 [4, 8, 16, 16], P('sect'), may hold values from -0.5 to 0.5
- edge_env: float32 [128, 128], replicated, may hold values from -0.5 to 0.5
Outputs:
- updated: bfloat16 [4, 4096, 2048], P('sect', 'blk')
- outgoing: float32 [4, 128, 128], P('sect')
Inputs may be any that keep to these rules, and one draw needn't show every extreme that they name: `sector_ids`: within each section the sector numbers never fall along the rows; each sector holds 1 to 2560 rows and one holds exactly 2560.
All inputs are finite; a program needn't handle non-finite values.
Results may differ from a plain program's by a relative error of at most 0.00165.
Values may be sent and summed in bfloat16 or wider, within the bound.
No kernel may reach another device: no remote copies, remote signals or barrier semaphores. Data moves between devices by JAX's collectives and lax.ppermute only.
A program may use at most 128 MiB of HBM per device.

v0:
```python
import jax
import jax.numpy as jnp
from jax import lax
from jax.sharding import PartitionSpec as P


def shifted(array, axis, by):
    peers = lax.axis_size(axis)
    pairs = [(i, i + by) for i in range(peers) if 0 <= i + by < peers]
    return lax.ppermute(array, axis, pairs)


def matprod(first, second):
    return jnp.dot(first, second, precision=lax.Precision.HIGHEST)


def per_device(theta, left_env, sector_ids, local_ops, edge_env):
    rows_dev = theta.shape[1]
    width = theta.shape[2]
    chain_w = left_env.shape[1]
    phys = local_ops.shape[2]
    cols = width // phys
    theta_loc = theta[0]
    env_loc = left_env[0]
    sec_all = sector_ids[0]
    ops_loc = local_ops[0]
    my_block = lax.axis_index("blk")
    row_start = my_block * rows_dev
    my_sec = lax.dynamic_slice_in_dim(sec_all, row_start, rows_dev, 0)
    same = my_sec[:, None] == sec_all[None, :]
    masked = jnp.where(same[None, :, :], env_loc, jnp.zeros_like(env_loc))
    applied = jnp.einsum(
        "wij,jx->wix",
        masked,
        lax.all_gather(theta_loc, "blk", axis=0, tiled=True),
        preferred_element_type=jnp.float32,
    )
    applied = applied.reshape(chain_w, rows_dev, phys, cols)
    acted = jnp.einsum("wpq,wiqc->ipc", ops_loc, applied, precision=lax.Precision.HIGHEST)
    theta_f = theta_loc.astype(jnp.float32).reshape(rows_dev, phys, cols)
    partial_intersection = jnp.einsum(
        "ipc,ipd->cd", theta_f, acted, precision=lax.Precision.HIGHEST
    )
    intersection = lax.psum(partial_intersection, "blk")
    transfer = (
        intersection
        * jnp.sqrt(jnp.float32(cols))
        / jnp.sqrt(jnp.sum(intersection * intersection) + 1e-06)
    )
    sect_no = lax.axis_index("sect")
    incoming = edge_env
    for step_no in range(lax.axis_size("sect") - 1):
        leaving = matprod(incoming, transfer)
        passed = shifted(leaving, "sect", 1)
        incoming = jnp.where(sect_no == 0, edge_env, passed)
    outgoing = matprod(incoming, transfer)
    result = jnp.einsum("ipc,cd->ipd", acted, incoming, precision=lax.Precision.HIGHEST)
    updated = result.reshape(1, rows_dev, width).astype(jnp.bfloat16)
    return (updated, outgoing[None])


def solution(mesh):
    placed = (
        P("sect", "blk", None),
        P("sect", None, "blk", None),
        P("sect", None),
        P("sect", None, None, None),
        P(),
    )
    return jax.shard_map(
        per_device,
        mesh=mesh,
        in_specs=placed,
        out_specs=(P("sect", "blk", None), P("sect", None, None)),
        check_vma=False,
    )
```

profile of v0, /device:TPU:8, one launch (start us, length us, event | category | flops | bytes accessed | tf_op | source)
XLA Modules:
  0.0 271.1 jit_solution(17785318184022447140)
XLA Ops:
  7.2 0.0 copy-start
  7.2 0.0 all-gather.3.cloned.1.call-start
  7.2 0.7 all-gather.3.cloned.1.call-update
  7.9 0.0 all-reduce.2.cloned.1.call-start
  8.0 1.1 copy.21
  9.1 0.7 dynamic-slice_bitcast_fusion
  9.8 1.1 broadcast_compare_fusion
  10.9 74.4 %all-gather.3.cloned.1.call-done = bf16[1,4096,2048]{2,1,0:T(8,128)(2,1)} async-done(((bf16[1,128,2048]{2,1,0:T(8,128)(2,1)}), bf16[1,4096,2048]{2,1,0:T(8,128)(2,1)}) %all-gather.3.cloned.1.call-update) | async-done | bytes 16777232 | tf_op jit(solution)/shard_map/all_gather | solution.py:35
  85.2 15.1 %copy.20 = bf16[512,8,16,128]{3,2,1,0:T(8,128)(2,1)} copy(bf16[512,8,16,128]{3,1,2,0:T(8,128)(2,1)} %bitcast.44) | data formatting | bytes 33554432
  100.3 25.4 %fusion = f32[8,128,16,128]{3,1,2,0:T(8,128)} fusion(bf16[16,128,4096,1]{1,0,2,3:T(8,128)(2,1)} %bitcast.45, bf16[1,8,128,4096]{3,2,1,0:T(8,128)(2,1)} %param.6, pred[128,4096]{1,0:T(8,128)(4,1)S(1)} %broadcast_compare_fusion), kind=kOutput, calls=%fused_computation | convolution fusion | flops 17184063488 | bytes 34078720 | tf_op jit(solution)/shard_map/wij,jx->wix/dot_general | solution.py:32
  125.8 0.0 copy-done
  125.8 0.0 copy-start.1
  125.8 12.4 %fusion.8 = f32[128,16,128]{2,1,0:T(8,128)S(1)} fusion(f32[8,128,16,128]{3,1,2,0:T(8,128)} %fusion, f32[1,8,16,16]{3,2,1,0:T(8,128)S(1)} %copy-done), kind=kOutput, calls=%fused_computation.8 | convolution fusion | flops 402653184 | bytes 9445376 | tf_op jit(solution)/shard_map/wpq,wiqc->ipc/dot_general | solution.py:39
  138.2 1.6 convolution_bitcast_fusion
  139.8 0.0 all-reduce.2.cloned.1.call-update
  139.8 96.2 %all-reduce.2.cloned.1.call-done = f32[128,128]{0,1:T(8,128)} async-done(((f32[128,128]{0,1:T(8,128)}), f32[128,128]{0,1:T(8,128)}) %all-reduce.2.cloned.1.call-update) | async-done | bytes 65552 | tf_op jit(solution)/shard_map/psum | solution.py:44
  236.1 1.5 multiply_reduce_fusion
  238.2 0.0 copy-done.1
  238.2 1.1 convolution_bitcast_fusion.2
  239.3 3.4 %collective-permute-start = (f32[128,128]{1,0:T(8,128)S(1)}, f32[128,128]{1,0:T(8,128)S(1)}, u32[]{:S(2)}, u32[]{:S(2)}) collective-permute-start(f32[128,128]{1,0:T(8,128)S(1)} %convolution_bitcast_fusion.2), channel_id=1, source_target_pairs={{0,32},{32,64},{64,96},{1,33},{33,65},{65,97},{2,34},{34,66},{66,9... | collective-permute-start | bytes 196616 | tf_op jit(solution)/shard_map/ppermute | solution.py:10
  242.7 2.8 %collective-permute-done = f32[128,128]{1,0:T(8,128)S(1)} collective-permute-done((f32[128,128]{1,0:T(8,128)S(1)}, f32[128,128]{1,0:T(8,128)S(1)}, u32[]{:S(2)}, u32[]{:S(2)}) %collective-permute-start) | collective-permute-done | bytes 65568 | tf_op jit(solution)/shard_map/ppermute | solution.py:10
  245.6 1.1 fusion.16
  246.7 3.4 %collective-permute-start.1 = (f32[128,128]{1,0:T(8,128)S(1)}, f32[128,128]{1,0:T(8,128)S(1)}, u32[]{:S(2)}, u32[]{:S(2)}) collective-permute-start(f32[128,128]{1,0:T(8,128)S(1)} %fusion.16), channel_id=1, source_target_pairs={{0,32},{32,64},{64,96},{1,33},{33,65},{65,97},{2,34},{34,66},{66,9... | collective-permute-start | bytes 196616 | tf_op jit(solution)/shard_map/ppermute | solution.py:10
  250.1 2.8 %collective-permute-done.1 = f32[128,128]{1,0:T(8,128)S(1)} collective-permute-done((f32[128,128]{1,0:T(8,128)S(1)}, f32[128,128]{1,0:T(8,128)S(1)}, u32[]{:S(2)}, u32[]{:S(2)}) %collective-permute-start.1) | collective-permute-done | bytes 65568 | tf_op jit(solution)/shard_map/ppermute | solution.py:10
  252.8 1.1 fusion.14
  253.9 3.4 %collective-permute-start.2 = (f32[128,128]{1,0:T(8,128)S(1)}, f32[128,128]{1,0:T(8,128)S(1)}, u32[]{:S(2)}, u32[]{:S(2)}) collective-permute-start(f32[128,128]{1,0:T(8,128)S(1)} %fusion.14), channel_id=1, source_target_pairs={{0,32},{32,64},{64,96},{1,33},{33,65},{65,97},{2,34},{34,66},{66,9... | collective-permute-start | bytes 196616 | tf_op jit(solution)/shard_map/ppermute | solution.py:10
  257.3 2.8 %collective-permute-done.2 = f32[128,128]{1,0:T(8,128)S(1)} collective-permute-done((f32[128,128]{1,0:T(8,128)S(1)}, f32[128,128]{1,0:T(8,128)S(1)}, u32[]{:S(2)}, u32[]{:S(2)}) %collective-permute-start.2) | collective-permute-done | bytes 65568 | tf_op jit(solution)/shard_map/ppermute | solution.py:10
  260.1 1.4 convolution_convert_fusion
  261.5 1.0 copy.11
  262.5 1.7 convolution_bitcast_fusion.1
Async XLA Ops:
  7.2 118.6 %copy-start = (f32[1,8,16,16]{3,2,1,0:T(8,128)S(1)}, f32[1,8,16,16]{3,2,1,0:T(8,128)}, u32[]{:S(2)}) copy-start(f32[1,8,16,16]{3,2,1,0:T(8,128)} %param.8) | copy-start | bytes 24580
  7.2 78.1 %all-gather.3.cloned.1.call-start = ((), (), s32[]{:S(2)}) async-start(), calls=%async_computation.1 | async-start | bytes 17301504 | tf_op jit(solution)/shard_map/all_gather | solution.py:35
  7.9 228.1 %all-reduce.2.cloned.1.call-start = ((), (), s32[]{:S(2)}) async-start(), calls=%async_computation | async-start | bytes 131072 | tf_op jit(solution)/shard_map/psum | solution.py:44
  125.8 112.5 %copy-start.1 = (f32[128,128]{1,0:T(8,128)S(1)}, f32[128,128]{1,0:T(8,128)}, u32[]{:S(2)}) copy-start(f32[128,128]{1,0:T(8,128)} %param.9) | copy-start | bytes 196612
  239.3 6.2 %collective-permute-start = (f32[128,128]{1,0:T(8,128)S(1)}, f32[128,128]{1,0:T(8,128)S(1)}, u32[]{:S(2)}, u32[]{:S(2)}) collective-permute-start(f32[128,128]{1,0:T(8,128)S(1)} %convolution_bitcast_fusion.2), channel_id=1, source_target_pairs={{0,32},{32,64},{64,96},{1,33},{33,65},{65,97},{2,34},{34,66},{66,9... | collective-permute-start | bytes 196616 | tf_op jit(solution)/shard_map/ppermute | solution.py:10
  246.7 6.2 %collective-permute-start.1 = (f32[128,128]{1,0:T(8,128)S(1)}, f32[128,128]{1,0:T(8,128)S(1)}, u32[]{:S(2)}, u32[]{:S(2)}) collective-permute-start(f32[128,128]{1,0:T(8,128)S(1)} %fusion.16), channel_id=1, source_target_pairs={{0,32},{32,64},{64,96},{1,33},{33,65},{65,97},{2,34},{34,66},{66,9... | collective-permute-start | bytes 196616 | tf_op jit(solution)/shard_map/ppermute | solution.py:10
  253.9 6.2 %collective-permute-start.2 = (f32[128,128]{1,0:T(8,128)S(1)}, f32[128,128]{1,0:T(8,128)S(1)}, u32[]{:S(2)}, u32[]{:S(2)}) collective-permute-start(f32[128,128]{1,0:T(8,128)S(1)} %fusion.14), channel_id=1, source_target_pairs={{0,32},{32,64},{64,96},{1,33},{33,65},{65,97},{2,34},{34,66},{66,9... | collective-permute-start | bytes 196616 | tf_op jit(solution)/shard_map/ppermute | solution.py:10
Sparse Core Ops, SparseCore 0:
  10.2 74.9 all-gather.2
  139.9 96.0 all-reduce.1
where the time goes:
time: 272 us; the launch traced here: 271 us
  waiting for transfers between devices  180 us (66%)
  matrix products  45.9 us (17%)
  local copies, waits for them, and re-layouts  17.9 us (7%)
  between operations  14.8 us (5%)
  starting transfers between devices  10.2 us (4%)
    psum x1, waiting for transfers between devices, per_device(): intersection = lax.psum(partial_intersection, 'blk')  96.2 us
    all_gather x1, waiting for transfers between devices, per_device(): lax.all_gather(theta_loc, 'blk', axis=0, tiled=True)  74.4 us
    dot_general x1, matrix products, per_device(): jnp.einsum('wij,jx->wix', masked, lax.all_gather(theta_loc, 'blk', axis=0...  25.4 us
    unnamed x7, local copies, waits for them, and re-layouts  17.2 us
    dot_general x1, matrix products, per_device(): jnp.einsum('wpq,wiqc->ipc', ops_loc, applied, precision=lax.Precision.HIG...  12.4 us
    ppermute x3, starting transfers between devices, shifted(): return lax.ppermute(array, axis, pairs)  10.2 us
    ppermute x3, waiting for transfers between devices, shifted(): return lax.ppermute(array, axis, pairs)  8.33 us
  transfers between devices with their start and end apart: 5, of which 5 were waited for; matrix products, arithmetic and copies ran while one was open for 1% of the time, Pallas kernels for 0%

commit v1 on v0

--- a/solution.py
+++ b/solution.py
@@ -2,6 +2,14 @@
 import jax.numpy as jnp
 from jax import lax
 from jax.sharding import PartitionSpec as P
+
+
+def gather_by_exchange(shard, axis, dim):
+    peers = lax.axis_size(axis)
+    repeats = [peers if d == dim else 1 for d in range(shard.ndim)]
+    return lax.all_to_all(
+        jnp.tile(shard, repeats), axis, split_axis=dim, concat_axis=dim, tiled=True
+    )
 
 
 def shifted(array, axis, by):
@@ -32,7 +40,7 @@
     applied = jnp.einsum(
         "wij,jx->wix",
         masked,
-        lax.all_gather(theta_loc, "blk", axis=0, tiled=True),
+        gather_by_exchange(theta_loc, "blk", 0),
         preferred_element_type=jnp.float32,
     )
     applied = applied.reshape(chain_w, rows_dev, phys, cols)

time: 272 us -> 478 us (1.76)
  waiting for transfers between devices: 180 us -> 374 us
  starting transfers between devices: 10.2 us -> 18.6 us
  local copies, waits for them, and re-layouts: 17.9 us -> 23 us
    all_to_all x0 -> x1, waiting for transfers between devices: none -> 240 us  [gather_by_exchange(): lax.all_to_all(jnp.tile(shard, repeats), axis, split_axis=dim, concat_axi...]
    all_gather x1 -> x0, waiting for transfers between devices: 74.4 us -> none  [per_device(): lax.all_gather(theta_loc, 'blk', axis=0, tiled=True)]
    psum x1, waiting for transfers between devices: 96.2 us -> 126 us  [per_device(): intersection = lax.psum(partial_intersection, 'blk')]
    all_to_all x0 -> x1, starting transfers between devices: none -> 8.42 us  [gather_by_exchange(): lax.all_to_all(jnp.tile(shard, repeats), axis, split_axis=dim, concat_axi...]
    another operation x0 -> x1, local copies, waits for them, and re-layouts: none -> 6.82 us  [gather_by_exchange(): jnp.tile(shard, repeats)]
    unnamed x7 -> x11, local copies, waits for them, and re-layouts: 17.2 us -> 16.2 us
  transfers between devices with their start and end apart: 5 -> 5, of which waited for: 5 -> 5; matrix products, arithmetic and copies ran while one was open for 1% -> 0% of each run, Pallas kernels for 0% -> 0%
where the time goes in v1:
time: 478 us
  waiting for transfers between devices  374 us (78%)
  matrix products  45.9 us (10%)
  local copies, waits for them, and re-layouts  23 us (5%)
  starting transfers between devices  18.6 us (4%)
  between operations  14.8 us (3%)
    all_to_all x1, waiting for transfers between devices, gather_by_exchange(): lax.all_to_all(jnp.tile(shard, repeats), axis, split_axis=dim, concat_axi...  240 us
    psum x1, waiting for transfers between devices, per_device(): intersection = lax.psum(partial_intersection, 'blk')  126 us
    dot_general x1, matrix products, per_device(): jnp.einsum('wij,jx->wix', masked, gather_by_exchange(theta_loc, 'blk', 0)...  25.4 us
    unnamed x11, local copies, waits for them, and re-layouts  16.2 us
    dot_general x1, matrix products, per_device(): jnp.einsum('wpq,wiqc->ipc', ops_loc, applied, precision=lax.Precision.HIG...  12.4 us
    ppermute x3, starting transfers between devices, shifted(): return lax.ppermute(array, axis, pairs)  10.2 us
  transfers between devices with their start and end apart: 5, of which 5 were waited for; matrix products, arithmetic and copies ran while one was open for 0% of the time, Pallas kernels for 0%

profile of v1, /device:TPU:8, one launch (start us, length us, event | category | flops | bytes accessed | tf_op | source)
XLA Modules:
  0.0 477.8 jit_solution(15257883737034673962)
XLA Ops:
  7.2 0.0 copy-start
  7.2 6.8 %tile.9 = bf16[32,128,2048]{2,1,0:T(8,128)(2,1)} broadcast(bf16[128,2048]{1,0:T(8,128)(2,1)} %bitcast.46), dimensions={1,2} | broadcast | bytes 17301504 | tf_op jit(solution)/shard_map/tile | solution.py:11
  14.0 0.0 copy-start.1
  14.0 0.0 copy-start.3
  14.0 8.4 %all-to-all-start = ((bf16[32,128,2048]{2,1,0:T(8,128)(2,1)}), bf16[32,128,2048]{2,1,0:T(8,128)(2,1)}, u32[]{:S(2)}, u32[]{:S(2)}) async-start(bf16[32,128,2048]{2,1,0:T(8,128)(2,1)} %tile.9), calls=%async_computation | async-start | bytes 33554432 | tf_op jit(solution)/shard_map/all_to_all | solution.py:10
  22.4 0.0 all-reduce.2.cloned.1.call-start
  22.5 0.0 copy-done.1
  22.5 0.1 copy.21
  22.6 0.0 copy-done.3
  22.6 0.4 broadcast_compare_fusion
  23.0 239.6 %all-to-all-done = bf16[32,128,2048]{2,1,0:T(8,128)(2,1)} async-done(((bf16[32,128,2048]{2,1,0:T(8,128)(2,1)}), bf16[32,128,2048]{2,1,0:T(8,128)(2,1)}, u32[]{:S(2)}, u32[]{:S(2)}) %all-to-all-start) | async-done | bytes 16777248 | tf_op jit(solution)/shard_map/all_to_all | solution.py:10
  262.6 15.1 %copy.20 = bf16[512,8,16,128]{3,2,1,0:T(8,128)(2,1)} copy(bf16[512,8,16,128]{3,1,2,0:T(8,128)(2,1)} %bitcast.24) | data formatting | bytes 33554432
  277.7 25.4 %fusion = f32[8,128,16,128]{3,1,2,0:T(8,128)} fusion(bf16[16,128,4096,1]{1,0,2,3:T(8,128)(2,1)} %bitcast.45, bf16[1,8,128,4096]{3,2,1,0:T(8,128)(2,1)} %param.6, pred[128,4096]{1,0:T(8,128)(4,1)S(1)} %broadcast_compare_fusion), kind=kOutput, calls=%fused_computation | convolution fusion | flops 17184063488 | bytes 34078720 | tf_op jit(solution)/shard_map/wij,jx->wix/dot_general | solution.py:40
  303.1 0.0 copy-done
  303.1 0.0 copy-start.2
  303.1 12.4 %fusion.8 = f32[128,16,128]{2,1,0:T(8,128)S(1)} fusion(f32[8,128,16,128]{3,1,2,0:T(8,128)} %fusion, f32[1,8,16,16]{3,2,1,0:T(8,128)S(1)} %copy-done), kind=kOutput, calls=%fused_computation.8 | convolution fusion | flops 402653184 | bytes 9445376 | tf_op jit(solution)/shard_map/wpq,wiqc->ipc/dot_general | solution.py:47
  315.5 1.6 convolution_bitcast_fusion
  317.2 0.0 all-reduce.2.cloned.1.call-update
  317.2 125.6 %all-reduce.2.cloned.1.call-done = f32[128,128]{0,1:T(8,128)} async-done(((f32[128,128]{0,1:T(8,128)}), f32[128,128]{0,1:T(8,128)}) %all-reduce.2.cloned.1.call-update) | async-done | bytes 65552 | tf_op jit(solution)/shard_map/psum | solution.py:52
  442.8 1.5 multiply_reduce_fusion
  444.9 0.0 copy-done.2
  444.9 1.1 convolution_bitcast_fusion.2
  446.1 3.4 collective-permute-start
  449.5 2.8 collective-permute-done
  452.3 1.1 fusion.16
  453.4 3.4 collective-permute-start.1
  456.8 2.8 collective-permute-done.1
  459.5 1.1 fusion.14
  460.7 3.4 collective-permute-start.2
  464.1 2.8 collective-permute-done.2
  466.8 1.4 convolution_convert_fusion
  468.2 1.0 copy.11
  469.2 1.7 convolution_bitcast_fusion.1
  (1 shorter events, 0.0 us)
Async XLA Ops:
  7.2 296.0 %copy-start = (f32[1,8,16,16]{3,2,1,0:T(8,128)S(1)}, f32[1,8,16,16]{3,2,1,0:T(8,128)}, u32[]{:S(2)}) copy-start(f32[1,8,16,16]{3,2,1,0:T(8,128)} %param.8) | copy-start | bytes 24580
  14.0 8.5 %copy-start.1 = (bf16[1,128,2048]{2,1,0:T(8,128)(2,1)S(1)}, bf16[1,128,2048]{2,1,0:T(8,128)(2,1)}, u32[]{:S(2)}) copy-start(bf16[1,128,2048]{2,1,0:T(8,128)(2,1)} %param.5) | copy-start | bytes 1572868
  14.0 8.6 %copy-start.3 = (s32[1,4096]{1,0:T(1,128)S(1)}, s32[1,4096]{1,0:T(1,128)}, u32[]{:S(2)}) copy-start(s32[1,4096]{1,0:T(1,128)} %param.7) | copy-start | bytes 49156
  14.0 248.6 %all-to-all-start = ((bf16[32,128,2048]{2,1,0:T(8,128)(2,1)}), bf16[32,128,2048]{2,1,0:T(8,128)(2,1)}, u32[]{:S(2)}, u32[]{:S(2)}) async-start(bf16[32,128,2048]{2,1,0:T(8,128)(2,1)} %tile.9), calls=%async_computation | async-start | bytes 33554432 | tf_op jit(solution)/shard_map/all_to_all | solution.py:10
  22.4 420.4 %all-reduce.2.cloned.1.call-start = ((), (), s32[]{:S(2)}) async-start(), calls=%async_computation.1 | async-start | bytes 131072 | tf_op jit(solution)/shard_map/psum | solution.py:52
  303.1 141.8 %copy-start.2 = (f32[128,128]{1,0:T(8,128)S(1)}, f32[128,128]{1,0:T(8,128)}, u32[]{:S(2)}) copy-start(f32[128,128]{1,0:T(8,128)} %param.9) | copy-start | bytes 196612
  446.1 6.2 %collective-permute-start = (f32[128,128]{1,0:T(8,128)S(1)}, f32[128,128]{1,0:T(8,128)S(1)}, u32[]{:S(2)}, u32[]{:S(2)}) collective-permute-start(f32[128,128]{1,0:T(8,128)S(1)} %convolution_bitcast_fusion.2), channel_id=1, source_target_pairs={{0,32},{32,64},{64,96},{1,33},{33,65},{65,97},{2,34},{34,66},{66,9... | collective-permute-start | bytes 196616 | tf_op jit(solution)/shard_map/ppermute | solution.py:18
  453.4 6.2 %collective-permute-start.1 = (f32[128,128]{1,0:T(8,128)S(1)}, f32[128,128]{1,0:T(8,128)S(1)}, u32[]{:S(2)}, u32[]{:S(2)}) collective-permute-start(f32[128,128]{1,0:T(8,128)S(1)} %fusion.16), channel_id=1, source_target_pairs={{0,32},{32,64},{64,96},{1,33},{33,65},{65,97},{2,34},{34,66},{66,9... | collective-permute-start | bytes 196616 | tf_op jit(solution)/shard_map/ppermute | solution.py:18
  460.7 6.2 %collective-permute-start.2 = (f32[128,128]{1,0:T(8,128)S(1)}, f32[128,128]{1,0:T(8,128)S(1)}, u32[]{:S(2)}, u32[]{:S(2)}) collective-permute-start(f32[128,128]{1,0:T(8,128)S(1)} %fusion.14), channel_id=1, source_target_pairs={{0,32},{32,64},{64,96},{1,33},{33,65},{65,97},{2,34},{34,66},{66,9... | collective-permute-start | bytes 196616 | tf_op jit(solution)/shard_map/ppermute | solution.py:18
Sparse Core Ops, SparseCore 0:
  317.3 125.4 all-reduce.1
